TPU v7x, 32 devices: a whole 2x2x4 slice. The times are simulated.
32 devices in a mesh: grp: 8 (over z, x), rep: 4 (over y, core).
Axes of the slice: x: 2, y: 2, z: 4, core: 2. Of those that a mesh axis runs over, the one named last changes fastest.
Arguments:
- three_center: bfloat16 [4, 64, 32, 6, 4096], P('rep', 'grp'), may hold values from -2 to 2
- metric: bfloat16 [4, 64, 64], P('rep'), may hold values from -0.75 to 0.75
- occupied: bfloat16 [2048, 48], replicated, may hold values from -0.3125 to 0.3125
- nu_list: int32 [32, 6], replicated, may hold values from 0 to 31, as said below
- nu_count: int32 [32], replicated, may hold values from 1 to 6
- block_size: int32 [32], replicated, may hold values from 32 to 64
Outputs:
- exchange_matrix: float32 [2048, 2048], P('rep', 'grp')
Inputs may be any that keep to these rules, and one draw needn't show every extreme that they name: `nu_list`: entry 0 of row m is m itself; the other entries of a row are distinct blocks other than m.
All inputs are finite; a program needn't handle non-finite values.
Results may differ from a plain program's by a relative error of at most 0.0024.
Values may be sent and summed in bfloat16 or wider, within the bound.
No kernel may reach another device: no remote copies, remote signals or barrier semaphores. Data moves between devices by JAX's collectives and lax.ppermute only.
A program may use at most 192 MiB of HBM per device.

v0:
```python
import jax
import jax.numpy as jnp
from jax import lax
from jax.sharding import PartitionSpec as P

NB = 64
N_CHUNKS = 4


def body(three_center, metric, occupied, nu_list, nu_count, block_size):
    n_mu, knu = nu_list.shape
    n_occ = occupied.shape[1]
    aux_dev = three_center.shape[1]
    occ_c = n_occ // N_CHUNKS
    lanes = jnp.arange(NB, dtype=jnp.int32)
    row_live = lanes[None, :] < block_size[:, None]
    col_live = lanes[None, None, :] < block_size[nu_list][:, :, None]
    slot_live = jnp.arange(knu, dtype=jnp.int32)[None, :] < nu_count[:, None]
    mask = row_live[:, None, :, None] & col_live[:, :, None, :] & slot_live[:, :, None, None]
    blocks = three_center[0].reshape(aux_dev, n_mu, knu, NB, NB)
    masked = jnp.where(mask[None], blocks, jnp.zeros((), jnp.bfloat16))
    picked = occupied.reshape(n_mu, NB, N_CHUNKS, occ_c)[nu_list]
    half = jnp.einsum(
        "qmkab,mkbci->cqmai", masked, picked, preferred_element_type=jnp.float32
    ).astype(jnp.bfloat16)
    half = half.reshape(N_CHUNKS, aux_dev, n_mu, NB * occ_c)
    n_grp = lax.axis_size("grp")
    rows = n_mu * NB // n_grp
    start = lax.axis_index("grp") * rows
    term = None
    for c in range(N_CHUNKS):
        gathered = lax.all_gather(half[c], "grp", axis=0, tiled=True)
        n_aux = gathered.shape[0]
        gathered = gathered.reshape(n_aux, n_mu, NB, occ_c)
        orbital = jnp.einsum(
            "pq,qmai->mapi", metric[0], gathered, preferred_element_type=jnp.float32
        ).astype(jnp.bfloat16)
        orbital = orbital.reshape(n_mu * NB, n_aux * occ_c)
        mine = lax.dynamic_slice_in_dim(orbital, start, rows, axis=0)
        part = jnp.dot(orbital, mine.T, preferred_element_type=jnp.float32)
        term = part if term is None else term + part
    return lax.psum_scatter(term, "rep", scatter_dimension=0, tiled=True)


def solution(mesh):
    return jax.shard_map(
        body,
        mesh=mesh,
        in_specs=(P("rep", "grp", None, None, None), P("rep", None, None), P(), P(), P(), P()),
        out_specs=P("rep", "grp"),
        check_vma=False,
    )
```

profile of v0, /device:TPU:0, one launch (start us, length us, event | category | flops | bytes accessed | tf_op | source)
XLA Modules:
  0.0 872.6 jit_solution(10821817166071291102)
XLA Ops:
  6.6 34.4 %reshape_squeeze.3 = bf16[8,32,6,64,64]{4,3,1,2,0:T(8,128)(2,1)} reshape(bf16[1,8,32,6,4096]{4,2,3,1,0:T(8,128)(2,1)} %param.6) | data formatting | bytes 25165824 | tf_op jit(solution)/shard_map/reshape;squeeze | solution.py:20
  43.9 2.6 gather_fusion
  48.1 17.4 %fusion.4 = bf16[4,8,32,64,12]{3,4,1,0,2:T(8,128)(2,1)} fusion(bf16[8,32,6,64,64]{4,3,1,2,0:T(8,128)(2,1)} %reshape_squeeze.3, pred[32,6,64,64]{3,2,1,0:T(8,128)(4,1)S(1)} %and_and_fusion, bf16[32,6,64,4,12,1]{2,3,4,1,0,5:T(4,128)(2,1)S(1)} %bitcast.76), kind=kOutput, calls=%fused_computation.13 | convolution fusion | flops 611057664 | bytes 16121856 | tf_op jit(solution)/shard_map/qmkab,mkbci->cqmai/dot_general | solution.py:23
  65.4 4.3 fusion.22
  69.8 5.3 copy.31
  75.1 4.1 copy.35
  79.2 10.4 %all-gather.9.cloned.1.call-start = ((), (), s32[]{:S(2)}) async-start(), calls=%async_computation.3 | async-start | bytes 14155776 | tf_op jit(solution)/shard_map/all_gather | solution.py:32
  89.7 4.1 copy.39
  93.9 4.1 copy.43
  98.1 156.4 %all-gather.5.cloned.1.call-done = bf16[64,32,768]{1,0,2:T(8,128)(2,1)} async-done(((bf16[8,32,768]{1,0,2:T(8,128)(2,1)}), bf16[64,32,768]{1,0,2:T(8,128)(2,1)}) %all-gather.5.cloned.1.call-update) | async-done | bytes 3145744 | tf_op jit(solution)/shard_map/all_gather | solution.py:32
  254.5 15.7 %copy.33 = bf16[64,32,64,12]{0,2,3,1:T(8,128)(2,1)} copy(bf16[64,32,64,12]{1,0,3,2:T(8,128)(2,1)} %bitcast.77) | data formatting | bytes 6291456 | tf_op jit(solution)/shard_map/reshape | solution.py:34
  270.3 7.2 convert_bitcast_fusion.3
  277.5 9.4 %copy.34 = bf16[32,64,64,12]{1,0,3,2:T(8,128)(2,1)} copy(bf16[32,64,64,12]{2,1,3,0:T(8,128)(2,1)} %convert_bitcast_fusion.3) | data formatting | bytes 6291456 | tf_op jit(solution)/shard_map/convert_element_type | solution.py:37
  286.9 9.7 %reshape.85 = bf16[2048,768]{0,1:T(8,128)(2,1)} reshape(bf16[32,64,64,12]{1,0,3,2:T(8,128)(2,1)} %copy.34) | data formatting | bytes 6291456 | tf_op jit(solution)/shard_map/reshape | solution.py:38
  296.6 134.7 %all-gather.7.cloned.1.call-done = bf16[64,32,768]{1,0,2:T(8,128)(2,1)} async-done(((bf16[8,32,768]{1,0,2:T(8,128)(2,1)}), bf16[64,32,768]{1,0,2:T(8,128)(2,1)}) %all-gather.7.cloned.1.call-update) | async-done | bytes 3145744 | tf_op jit(solution)/shard_map/all_gather | solution.py:32
  431.4 15.8 %copy.37 = bf16[64,32,64,12]{0,2,3,1:T(8,128)(2,1)} copy(bf16[64,32,64,12]{1,0,3,2:T(8,128)(2,1)} %bitcast.78) | data formatting | bytes 6291456 | tf_op jit(solution)/shard_map/reshape | solution.py:34
  447.1 7.3 convert_bitcast_fusion.2
  454.4 9.4 %copy.38 = bf16[32,64,64,12]{1,0,3,2:T(8,128)(2,1)} copy(bf16[32,64,64,12]{2,1,3,0:T(8,128)(2,1)} %convert_bitcast_fusion.2) | data formatting | bytes 6291456 | tf_op jit(solution)/shard_map/convert_element_type | solution.py:37
  463.8 8.5 reshape.87
  472.3 135.9 %all-gather.9.cloned.1.call-done = bf16[64,32,768]{1,0,2:T(8,128)(2,1)} async-done(((bf16[8,32,768]{1,0,2:T(8,128)(2,1)}), bf16[64,32,768]{1,0,2:T(8,128)(2,1)}) %all-gather.9.cloned.1.call-update) | async-done | bytes 3145744 | tf_op jit(solution)/shard_map/all_gather | solution.py:32
  608.2 15.8 %copy.41 = bf16[64,32,64,12]{0,2,3,1:T(8,128)(2,1)} copy(bf16[64,32,64,12]{1,0,3,2:T(8,128)(2,1)} %bitcast.79) | data formatting | bytes 6291456 | tf_op jit(solution)/shard_map/reshape | solution.py:34
  624.0 7.2 convert_bitcast_fusion.1
  631.1 9.5 %copy.42 = bf16[32,64,64,12]{1,0,3,2:T(8,128)(2,1)} copy(bf16[32,64,64,12]{2,1,3,0:T(8,128)(2,1)} %convert_bitcast_fusion.1) | data formatting | bytes 6291456 | tf_op jit(solution)/shard_map/convert_element_type | solution.py:37
  640.6 9.7 %reshape.89 = bf16[2048,768]{0,1:T(8,128)(2,1)} reshape(bf16[32,64,64,12]{1,0,3,2:T(8,128)(2,1)} %copy.42) | data formatting | bytes 6291456 | tf_op jit(solution)/shard_map/reshape | solution.py:38
  650.4 134.5 %all-gather.11.cloned.1.call-done = bf16[64,32,768]{1,0,2:T(8,128)(2,1)} async-done(((bf16[8,32,768]{1,0,2:T(8,128)(2,1)}), bf16[64,32,768]{1,0,2:T(8,128)(2,1)}) %all-gather.11.cloned.1.call-update) | async-done | bytes 3145744 | tf_op jit(solution)/shard_map/all_gather | solution.py:32
  784.9 15.5 %copy.45 = bf16[64,32,64,12]{0,2,3,1:T(8,128)(2,1)} copy(bf16[64,32,64,12]{1,0,3,2:T(8,128)(2,1)} %bitcast.80) | data formatting | bytes 6291456 | tf_op jit(solution)/shard_map/reshape | solution.py:34
  800.3 7.2 convert_bitcast_fusion
  807.6 9.4 %copy.46 = bf16[32,64,64,12]{1,0,3,2:T(8,128)(2,1)} copy(bf16[32,64,64,12]{2,1,3,0:T(8,128)(2,1)} %convert_bitcast_fusion) | data formatting | bytes 6291456 | tf_op jit(solution)/shard_map/convert_element_type | solution.py:37
  817.0 9.7 %reshape.91 = bf16[2048,768]{0,1:T(8,128)(2,1)} reshape(bf16[32,64,64,12]{1,0,3,2:T(8,128)(2,1)} %copy.46) | data formatting | bytes 6291456 | tf_op jit(solution)/shard_map/reshape | solution.py:38
  826.7 3.0 fusion.11
  833.5 2.5 convolution_add_fusion
  836.0 29.8 %reduce-scatter.2.cloned.1.call-done = f32[512,256]{1,0:T(8,128)} async-done(((f32[2048,256]{1,0:T(8,128)}), f32[512,256]{1,0:T(8,128)}) %reduce-scatter.2.cloned.1.call-update) | async-done | bytes 524304 | tf_op jit(solution)/shard_map/reduce_scatter | solution.py:42
  (37 shorter events, 8.4 us)
Async XLA Ops:
  6.5 263.7 %copy-start = (bf16[1,64,64]{2,1,0:T(8,128)(2,1)S(1)}, bf16[1,64,64]{2,1,0:T(8,128)(2,1)}, u32[]{:S(2)}) copy-start(bf16[1,64,64]{2,1,0:T(8,128)(2,1)} %param.7) | copy-start | bytes 24580
  6.5 34.5 %copy-start.6 = (s32[32]{0:T(128)S(1)}, s32[32]{0:T(128)}, u32[]{:S(2)}) copy-start(s32[32]{0:T(128)} %param.10) | copy-start | bytes 388
  6.5 34.5 %copy-start.5 = (s32[32,6]{0,1:T(8,128)S(1)}, s32[32,6]{0,1:T(8,128)}, u32[]{:S(2)}) copy-start(s32[32,6]{0,1:T(8,128)} %param.9) | copy-start | bytes 2308
  6.5 34.8 %copy-start.1 = (s32[32]{0:T(128)S(1)}, s32[32]{0:T(128)}, u32[]{:S(2)}) copy-start(s32[32]{0:T(128)} %param.11) | copy-start | bytes 388
  6.5 248.0 %all-gather.5.cloned.1.call-start = ((), (), s32[]{:S(2)}) async-start(), calls=%async_computation.1 | async-start | bytes 14155776 | tf_op jit(solution)/shard_map/all_gather | solution.py:32
  41.4 1.8 copy-start.4
  75.1 356.3 %all-gather.7.cloned.1.call-start = ((), (), s32[]{:S(2)}) async-start(), calls=%async_computation.2 | async-start | bytes 14155776 | tf_op jit(solution)/shard_map/all_gather | solution.py:32
  79.2 528.9 %all-gather.9.cloned.1.call-start = ((), (), s32[]{:S(2)}) async-start(), calls=%async_computation.3 | async-start | bytes 14155776 | tf_op jit(solution)/shard_map/all_gather | solution.py:32
  93.8 691.1 %all-gather.11.cloned.1.call-start = ((), (), s32[]{:S(2)}) async-start(), calls=%async_computation.4 | async-start | bytes 14155776 | tf_op jit(solution)/shard_map/all_gather | solution.py:32
  98.0 767.7 %reduce-scatter.2.cloned.1.call-start = ((), (), s32[]{:S(2)}) async-start(), calls=%async_computation.5 | async-start | bytes 2621440 | tf_op jit(solution)/shard_map/reduce_scatter | solution.py:42
  829.7 1.9 copy-start.2
  831.6 1.9 copy-start.3
Sparse Core Ops, SparseCore 0:
  75.2 179.2 all-gather.4
  256.6 174.7 all-gather.6
  433.4 174.7 all-gather.8
  610.1 174.7 all-gather.10
  836.1 29.6 reduce-scatter.1
where the time goes:
time: 885 us; the launch traced here: 873 us
  waiting for transfers between devices  591 us (67%)
  local copies, waits for them, and re-layouts  201 us (23%)
  matrix products  53.9 us (6%)
  between operations  13.7 us (2%)
  starting transfers between devices  10.6 us (1%)
    all_gather x4, waiting for transfers between devices, body(): gathered = lax.all_gather(half[c], 'grp', axis=0, tiled=True)  562 us
    reshape x4, local copies, waits for them, and re-layouts, body(): gathered = gathered.reshape(n_aux, n_mu, NB, occ_c)  62.7 us
    reshape x4, local copies, waits for them, and re-layouts, body(): orbital = orbital.reshape(n_mu * NB, n_aux * occ_c)  37.7 us
    convert_element_type x4, local copies, waits for them, and re-layouts, body(): orbital = jnp.einsum('pq,qmai->mapi', metric[0], gathered, preferred_elem...  37.7 us
    another operation x1, local copies, waits for them, and re-layouts, body(): blocks = three_center[0].reshape(aux_dev, n_mu, knu, NB, NB)  34.4 us
    reduce_scatter x1, waiting for transfers between devices, body(): return lax.psum_scatter(term, 'rep', scatter_dimension=0, tiled=True)  29.8 us
    dot_general x4, matrix products, body(): jnp.einsum('pq,qmai->mapi', metric[0], gathered, preferred_element_type=j...  28.9 us
    slice x5, local copies, waits for them, and re-layouts, body(): gathered = lax.all_gather(half[c], 'grp', axis=0, tiled=True)  22 us
  transfers between devices with their start and end apart: 5, of which 5 were waited for; matrix products, arithmetic and copies ran while one was open for 16% of the time, Pallas kernels for 0%

commit v1 on v0

--- a/solution.py
+++ b/solution.py
@@ -29,7 +29,16 @@
     start = lax.axis_index("grp") * rows
     term = None
     for c in range(N_CHUNKS):
-        gathered = lax.all_gather(half[c], "grp", axis=0, tiled=True)
+        ways = lax.axis_size("grp")
+        up = [(d, (d + 1) % ways) for d in range(ways)]
+        down = [(d, (d - 1) % ways) for d in range(ways)]
+        earlier, later = ([half[c]], [half[c]])
+        for _ in range(ways // 2):
+            earlier.append(lax.ppermute(earlier[-1], "grp", up))
+        for _ in range((ways - 1) // 2):
+            later.append(lax.ppermute(later[-1], "grp", down))
+        line = jnp.concatenate([*earlier[::-1], *later[1:]], axis=0)
+        gathered = jnp.roll(line, (lax.axis_index("grp") - ways // 2) * half[c].shape[0], axis=0)
         n_aux = gathered.shape[0]
         gathered = gathered.reshape(n_aux, n_mu, NB, occ_c)
         orbital = jnp.einsum(

time: 885 us -> 572 us (0.65)
  waiting for transfers between devices: 591 us -> 187 us
  starting transfers between devices: 10.6 us -> 57.7 us
  matrix products: 53.9 us -> 76.3 us
  local copies, waits for them, and re-layouts: 201 us -> 214 us
  other arithmetic: 1.82 us -> 13.1 us
    all_gather x4 -> x0, waiting for transfers between devices: 562 us -> none  [body(): gathered = lax.all_gather(half[c], 'grp', axis=0, tiled=True)]
    ppermute x0 -> x28, waiting for transfers between devices: none -> 156 us  [the longest x16 122 us: body(): earlier.append(lax.ppermute(earlier[-1], 'grp', up))]
    unnamed x14 -> x56, local copies, waits for them, and re-layouts: 1.61 us -> 67.1 us
    reshape x4 -> x0, local copies, waits for them, and re-layouts: 62.7 us -> none  [body(): gathered = gathered.reshape(n_aux, n_mu, NB, occ_c)]
    ppermute x0 -> x28, starting transfers between devices: none -> 57.7 us  [the longest x12 34.6 us: body(): later.append(lax.ppermute(later[-1], 'grp', down))]
    dot_general x4, matrix products: 28.9 us -> 51.2 us  [body(): jnp.einsum('pq,qmai->mapi', metric[0], gathered, preferred_element_type=j...]
    all_gather x4 -> x0, starting transfers between devices: 10.5 us -> none  [body(): gathered = lax.all_gather(half[c], 'grp', axis=0, tiled=True)]
    concatenate x0 -> x2, other arithmetic: none -> 9.33 us  [body(): jnp.roll(line, (lax.axis_index('grp') - ways // 2) * half[c].shape[0], ax...]
  transfers between devices with their start and end apart: 5 -> 29, of which waited for: 5 -> 18; matrix products, arithmetic and copies ran while one was open for 16% -> 15% of each run, Pallas kernels for 0% -> 0%
where the time goes in v1:
time: 572 us; the launch traced here: 561 us
  local copies, waits for them, and re-layouts  214 us (37%)
  waiting for transfers between devices  187 us (33%)
  matrix products  76.3 us (13%)
  starting transfers between devices  57.7 us (10%)
  between operations  14.1 us (2%)
  other arithmetic  13.1 us (2%)
    ppermute x16, waiting for transfers between devices, body(): earlier.append(lax.ppermute(earlier[-1], 'grp', up))  122 us
    unnamed x56, local copies, waits for them, and re-layouts  67.1 us
    dot_general x4, matrix products, body(): jnp.einsum('pq,qmai->mapi', metric[0], gathered, preferred_element_type=j...  51.2 us
    reshape x4, local copies, waits for them, and re-layouts, body(): orbital = orbital.reshape(n_mu * NB, n_aux * occ_c)  38.3 us
    convert_element_type x4, local copies, waits for them, and re-layouts, body(): orbital = jnp.einsum('pq,qmai->mapi', metric[0], gathered, preferred_elem...  37.9 us
    ppermute x12, starting transfers between devices, body(): later.append(lax.ppermute(later[-1], 'grp', down))  34.6 us
    another operation x1, local copies, waits for them, and re-layouts, body(): blocks = three_center[0].reshape(aux_dev, n_mu, knu, NB, NB)  34.4 us
    ppermute x12, waiting for transfers between devices, body(): later.append(lax.ppermute(later[-1], 'grp', down))  34.2 us
  transfers between devices with their start and end apart: 29, of which 18 were waited for; matrix products, arithmetic and copies ran while one was open for 15% of the time, Pallas kernels for 0%

profile of v1, /device:TPU:0, one launch (start us, length us, event | category | flops | bytes accessed | tf_op | source)
XLA Modules:
  0.0 561.4 jit_solution(6007128741193691033)
XLA Ops:
  14.1 34.4 %reshape_squeeze.3 = bf16[8,32,6,64,64]{4,3,1,2,0:T(8,128)(2,1)} reshape(bf16[1,8,32,6,4096]{4,2,3,1,0:T(8,128)(2,1)} %param.8) | data formatting | bytes 25165824 | tf_op jit(solution)/shard_map/reshape;squeeze | solution.py:20
  50.0 17.4 %fusion.12 = bf16[4,8,32,64,12]{3,4,1,0,2:T(8,128)(2,1)} fusion(bf16[8,32,6,64,64]{4,3,1,2,0:T(8,128)(2,1)} %reshape_squeeze.3, pred[32,6,64,64]{3,2,1,0:T(8,128)(4,1)S(1)} %and_and_fusion, bf16[32,6,64,4,12,1]{2,3,4,1,0,5:T(4,128)(2,1)S(1)} %bitcast.72), kind=kOutput, calls=%fused_computation.29 | convolution fusion | flops 611057664 | bytes 16121856 | tf_op jit(solution)/shard_map/qmkab,mkbci->cqmai/dot_general | solution.py:23
  94.4 8.4 %collective-permute-done.7 = bf16[8,32,768]{2,1,0:T(8,128)(2,1)} collective-permute-done((bf16[8,32,768]{2,1,0:T(8,128)(2,1)S(1)}, bf16[8,32,768]{2,1,0:T(8,128)(2,1)}, u32[]{:S(2)}, u32[]{:S(2)}) %collective-permute-start.7) | collective-permute-done | bytes 393248 | tf_op jit(solution)/shard_map/ppermute | solution.py:37
  102.8 8.4 %collective-permute-done.1 = bf16[8,32,768]{2,1,0:T(8,128)(2,1)} collective-permute-done((bf16[8,32,768]{2,1,0:T(8,128)(2,1)}, bf16[8,32,768]{2,1,0:T(8,128)(2,1)}, u32[]{:S(2)}, u32[]{:S(2)}) %collective-permute-start.1) | collective-permute-done | bytes 393248 | tf_op jit(solution)/shard_map/ppermute | solution.py:37
  119.7 8.4 %collective-permute-done.2 = bf16[8,32,768]{2,1,0:T(8,128)(2,1)} collective-permute-done((bf16[8,32,768]{2,1,0:T(8,128)(2,1)}, bf16[8,32,768]{2,1,0:T(8,128)(2,1)}, u32[]{:S(2)}, u32[]{:S(2)}) %collective-permute-start.2) | collective-permute-done | bytes 393248 | tf_op jit(solution)/shard_map/ppermute | solution.py:37
  142.3 16.0 %collective-permute-done.9 = bf16[8,32,768]{2,1,0:T(8,128)(2,1)} collective-permute-done((bf16[8,32,768]{2,1,0:T(8,128)(2,1)}, bf16[8,32,768]{2,1,0:T(8,128)(2,1)}, u32[]{:S(2)}, u32[]{:S(2)}) %collective-permute-start.9) | collective-permute-done | bytes 393248 | tf_op jit(solution)/shard_map/ppermute | solution.py:37
  172.8 13.5 %collective-permute-done.25 = bf16[8,32,768]{2,1,0:T(8,128)(2,1)S(1)} collective-permute-done((bf16[8,32,768]{2,1,0:T(8,128)(2,1)S(1)}, bf16[8,32,768]{2,1,0:T(8,128)(2,1)S(1)}, u32[]{:S(2)}, u32[]{:S(2)}) %collective-permute-start.25) | collective-permute-done | bytes 393248 | tf_op jit(solution)/shard_map/ppermute | solution.py:39
  196.7 20.6 %collective-permute-done.10 = bf16[8,32,768]{2,1,0:T(8,128)(2,1)} collective-permute-done((bf16[8,32,768]{2,1,0:T(8,128)(2,1)}, bf16[8,32,768]{2,1,0:T(8,128)(2,1)}, u32[]{:S(2)}, u32[]{:S(2)}) %collective-permute-start.10) | collective-permute-done | bytes 393248 | tf_op jit(solution)/shard_map/ppermute | solution.py:37
  230.3 6.5 %collective-permute-done.26 = bf16[8,32,768]{2,1,0:T(8,128)(2,1)S(1)} collective-permute-done((bf16[8,32,768]{2,1,0:T(8,128)(2,1)S(1)}, bf16[8,32,768]{2,1,0:T(8,128)(2,1)S(1)}, u32[]{:S(2)}, u32[]{:S(2)}) %collective-permute-start.26) | collective-permute-done | bytes 393248 | tf_op jit(solution)/shard_map/ppermute | solution.py:39
  237.5 13.4 %collective-permute-done.22 = bf16[8,32,768]{2,1,0:T(8,128)(2,1)S(1)} collective-permute-done((bf16[8,32,768]{2,1,0:T(8,128)(2,1)S(1)}, bf16[8,32,768]{2,1,0:T(8,128)(2,1)S(1)}, u32[]{:S(2)}, u32[]{:S(2)}) %collective-permute-start.22) | collective-permute-done | bytes 393248 | tf_op jit(solution)/shard_map/ppermute | solution.py:37
  270.1 8.9 %collective-permute-done.5 = bf16[8,32,768]{2,1,0:T(8,128)(2,1)} collective-permute-done((bf16[8,32,768]{2,1,0:T(8,128)(2,1)S(1)}, bf16[8,32,768]{2,1,0:T(8,128)(2,1)}, u32[]{:S(2)}, u32[]{:S(2)}) %collective-permute-start.5) | collective-permute-done | bytes 393248 | tf_op jit(solution)/shard_map/ppermute | solution.py:39
  279.6 13.4 %collective-permute-done.23 = bf16[8,32,768]{2,1,0:T(8,128)(2,1)S(1)} collective-permute-done((bf16[8,32,768]{2,1,0:T(8,128)(2,1)S(1)}, bf16[8,32,768]{2,1,0:T(8,128)(2,1)S(1)}, u32[]{:S(2)}, u32[]{:S(2)}) %collective-permute-start.23) | collective-permute-done | bytes 393248 | tf_op jit(solution)/shard_map/ppermute | solution.py:37
  293.0 9.7 %collective-permute-start.6 = (bf16[8,32,768]{2,1,0:T(8,128)(2,1)}, bf16[8,32,768]{2,1,0:T(8,128)(2,1)}, u32[]{:S(2)}, u32[]{:S(2)}) collective-permute-start(bf16[8,32,768]{2,1,0:T(8,128)(2,1)} %collective-permute-done.5), channel_id=1, source_target_pairs={{0,28},{4,0},{8,4},{12,8},{16,12},{20,16},{24,20},{28,24},{1,29},{... | collective-permute-start | bytes 1179656 | tf_op jit(solution)/shard_map/ppermute | solution.py:39
  302.8 6.0 %collective-permute-done.17 = bf16[8,32,768]{2,1,0:T(8,128)(2,1)S(1)} collective-permute-done((bf16[8,32,768]{2,1,0:T(8,128)(2,1)S(1)}, bf16[8,32,768]{2,1,0:T(8,128)(2,1)S(1)}, u32[]{:S(2)}, u32[]{:S(2)}) %collective-permute-start.17) | collective-permute-done | bytes 393248 | tf_op jit(solution)/shard_map/ppermute | solution.py:37
  312.9 9.0 %collective-permute-done.24 = bf16[8,32,768]{2,1,0:T(8,128)(2,1)S(1)} collective-permute-done((bf16[8,32,768]{2,1,0:T(8,128)(2,1)S(1)}, bf16[8,32,768]{2,1,0:T(8,128)(2,1)S(1)}, u32[]{:S(2)}, u32[]{:S(2)}) %collective-permute-start.24) | collective-permute-done | bytes 393248 | tf_op jit(solution)/shard_map/ppermute | solution.py:37
  325.9 11.3 %copy.88 = bf16[64,32,768]{0,1,2:T(8,128)(2,1)} copy(bf16[64,32,768]{2,1,0:T(8,128)(2,1)S(1)} %get-tuple-element.10) | data formatting | bytes 6291456
  337.1 12.8 %convert_bitcast_fusion = bf16[32,64,64,12]{2,1,3,0:T(8,128)(2,1)} fusion(bf16[64,32,64,12]{0,1,3,2:T(8,128)(2,1)} %bitcast.73, bf16[1,64,64]{2,1,0:T(8,128)(2,1)S(1)} %copy-done), kind=kOutput, calls=%fused_computation.24 | convolution fusion | flops 202899456 | bytes 6299648 | tf_op jit(solution)/shard_map/pq,qmai->mapi/dot_general | solution.py:44
  352.5 9.4 %copy.78 = bf16[32,64,64,12]{1,0,3,2:T(8,128)(2,1)} copy(bf16[32,64,64,12]{2,1,3,0:T(8,128)(2,1)} %convert_bitcast_fusion) | data formatting | bytes 6291456 | tf_op jit(solution)/shard_map/convert_element_type | solution.py:46
  361.9 8.6 %reshape.91 = bf16[2048,768]{0,1:T(8,128)(2,1)S(1)} reshape(bf16[32,64,64,12]{1,0,3,2:T(8,128)(2,1)} %copy.78) | data formatting | bytes 6291456 | tf_op jit(solution)/shard_map/reshape | solution.py:47
  382.6 12.2 %copy.86 = bf16[64,32,768]{0,1,2:T(8,128)(2,1)} copy(bf16[64,32,768]{2,1,0:T(8,128)(2,1)} %get-tuple-element.12) | data formatting | bytes 6291456
  394.7 12.8 %convert_bitcast_fusion.2 = bf16[32,64,64,12]{2,1,3,0:T(8,128)(2,1)} fusion(bf16[64,32,64,12]{0,1,3,2:T(8,128)(2,1)} %bitcast.74, bf16[1,64,64]{2,1,0:T(8,128)(2,1)S(1)} %copy-done), kind=kOutput, calls=%fused_computation.26 | convolution fusion | flops 202899456 | bytes 6299648 | tf_op jit(solution)/shard_map/pq,qmai->mapi/dot_general | solution.py:44
  407.5 9.6 %copy.64 = bf16[32,64,64,12]{1,0,3,2:T(8,128)(2,1)} copy(bf16[32,64,64,12]{2,1,3,0:T(8,128)(2,1)} %convert_bitcast_fusion.2) | data formatting | bytes 6291456 | tf_op jit(solution)/shard_map/convert_element_type | solution.py:46
  417.1 9.7 %reshape.87 = bf16[2048,768]{0,1:T(8,128)(2,1)} reshape(bf16[32,64,64,12]{1,0,3,2:T(8,128)(2,1)} %copy.64) | data formatting | bytes 6291456 | tf_op jit(solution)/shard_map/reshape | solution.py:47
  426.9 12.2 %copy.87 = bf16[64,32,768]{0,1,2:T(8,128)(2,1)} copy(bf16[64,32,768]{2,1,0:T(8,128)(2,1)} %get-tuple-element.11) | data formatting | bytes 6291456
  439.0 12.8 %convert_bitcast_fusion.1 = bf16[32,64,64,12]{2,1,3,0:T(8,128)(2,1)} fusion(bf16[64,32,64,12]{0,1,3,2:T(8,128)(2,1)} %bitcast.75, bf16[1,64,64]{2,1,0:T(8,128)(2,1)S(1)} %copy-done), kind=kOutput, calls=%fused_computation.25 | convolution fusion | flops 202899456 | bytes 6299648 | tf_op jit(solution)/shard_map/pq,qmai->mapi/dot_general | solution.py:44
  451.8 9.4 %copy.71 = bf16[32,64,64,12]{1,0,3,2:T(8,128)(2,1)} copy(bf16[32,64,64,12]{2,1,3,0:T(8,128)(2,1)} %convert_bitcast_fusion.1) | data formatting | bytes 6291456 | tf_op jit(solution)/shard_map/convert_element_type | solution.py:46
  461.2 10.1 %reshape.89 = bf16[2048,768]{0,1:T(8,128)(2,1)} reshape(bf16[32,64,64,12]{1,0,3,2:T(8,128)(2,1)} %copy.71) | data formatting | bytes 6291456 | tf_op jit(solution)/shard_map/reshape | solution.py:47
  471.4 12.2 %copy.85 = bf16[64,32,768]{0,1,2:T(8,128)(2,1)} copy(bf16[64,32,768]{2,1,0:T(8,128)(2,1)} %get-tuple-element.13) | data formatting | bytes 6291456
  483.5 12.8 %convert_bitcast_fusion.3 = bf16[32,64,64,12]{2,1,3,0:T(8,128)(2,1)} fusion(bf16[64,32,64,12]{0,1,3,2:T(8,128)(2,1)} %bitcast.76, bf16[1,64,64]{2,1,0:T(8,128)(2,1)S(1)} %copy-done), kind=kOutput, calls=%fused_computation.27 | convolution fusion | flops 202899456 | bytes 6299648 | tf_op jit(solution)/shard_map/pq,qmai->mapi/dot_general | solution.py:44
  496.3 9.4 %copy.57 = bf16[32,64,64,12]{1,0,3,2:T(8,128)(2,1)} copy(bf16[32,64,64,12]{2,1,3,0:T(8,128)(2,1)} %convert_bitcast_fusion.3) | data formatting | bytes 6291456 | tf_op jit(solution)/shard_map/convert_element_type | solution.py:46
  505.7 9.9 %reshape.85 = bf16[2048,768]{0,1:T(8,128)(2,1)} reshape(bf16[32,64,64,12]{1,0,3,2:T(8,128)(2,1)} %copy.57) | data formatting | bytes 6291456 | tf_op jit(solution)/shard_map/reshape | solution.py:47
  524.2 30.1 %reduce-scatter.2.cloned.1.call-done = f32[512,256]{1,0:T(8,128)} async-done(((f32[2048,256]{1,0:T(8,128)}), f32[512,256]{1,0:T(8,128)}) %reduce-scatter.2.cloned.1.call-update) | async-done | bytes 524304 | tf_op jit(solution)/shard_map/reduce_scatter | solution.py:51
  (129 shorter events, 147.8 us)
Async XLA Ops:
  6.5 330.6 %copy-start = (bf16[1,64,64]{2,1,0:T(8,128)(2,1)S(1)}, bf16[1,64,64]{2,1,0:T(8,128)(2,1)}, u32[]{:S(2)}) copy-start(bf16[1,64,64]{2,1,0:T(8,128)(2,1)} %param.9) | copy-start | bytes 24580
  6.5 547.8 %reduce-scatter.2.cloned.1.call-start = ((), (), s32[]{:S(2)}) async-start(), calls=%async_computation.1 | async-start | bytes 2621440 | tf_op jit(solution)/shard_map/reduce_scatter | solution.py:51
  78.0 16.4 %collective-permute-start = (bf16[8,32,768]{2,1,0:T(8,128)(2,1)S(1)}, bf16[8,32,768]{2,1,0:T(8,128)(2,1)}, u32[]{:S(2)}, u32[]{:S(2)}) collective-permute-start(bf16[8,32,768]{2,1,0:T(8,128)(2,1)S(1)} %copy.52), channel_id=1, source_target_pairs={{0,4},{4,8},{8,12},{12,16},{16,20},{20,24},{24,28},{28,0},{1,5},{5... | collective-permute-start | bytes 1179656 | tf_op jit(solution)/shard_map/ppermute | solution.py:37
  87.2 15.6 %collective-permute-start.7 = (bf16[8,32,768]{2,1,0:T(8,128)(2,1)S(1)}, bf16[8,32,768]{2,1,0:T(8,128)(2,1)}, u32[]{:S(2)}, u32[]{:S(2)}) collective-permute-start(bf16[8,32,768]{2,1,0:T(8,128)(2,1)S(1)} %copy.59), channel_id=1, source_target_pairs={{0,4},{4,8},{8,12},{12,16},{16,20},{20,24},{24,28},{28,0},{1,5},{5... | collective-permute-start | bytes 1179656 | tf_op jit(solution)/shard_map/ppermute | solution.py:37
  94.4 16.9 %collective-permute-start.1 = (bf16[8,32,768]{2,1,0:T(8,128)(2,1)}, bf16[8,32,768]{2,1,0:T(8,128)(2,1)}, u32[]{:S(2)}, u32[]{:S(2)}) collective-permute-start(bf16[8,32,768]{2,1,0:T(8,128)(2,1)} %collective-permute-done), channel_id=1, source_target_pairs={{0,4},{4,8},{8,12},{12,16},{16,20},{20,24},{24,28},{28,0},{1,5},{5... | collective-permute-start | bytes 1179656 | tf_op jit(solution)/shard_map/ppermute | solution.py:37
  102.8 16.9 %collective-permute-start.8 = (bf16[8,32,768]{2,1,0:T(8,128)(2,1)}, bf16[8,32,768]{2,1,0:T(8,128)(2,1)}, u32[]{:S(2)}, u32[]{:S(2)}) collective-permute-start(bf16[8,32,768]{2,1,0:T(8,128)(2,1)} %collective-permute-done.7), channel_id=1, source_target_pairs={{0,4},{4,8},{8,12},{12,16},{16,20},{20,24},{24,28},{28,0},{1,5},{5... | collective-permute-start | bytes 1179656 | tf_op jit(solution)/shard_map/ppermute | solution.py:37
  111.2 16.9 %collective-permute-start.2 = (bf16[8,32,768]{2,1,0:T(8,128)(2,1)}, bf16[8,32,768]{2,1,0:T(8,128)(2,1)}, u32[]{:S(2)}, u32[]{:S(2)}) collective-permute-start(bf16[8,32,768]{2,1,0:T(8,128)(2,1)} %collective-permute-done.1), channel_id=1, source_target_pairs={{0,4},{4,8},{8,12},{12,16},{16,20},{20,24},{24,28},{28,0},{1,5},{5... | collective-permute-start | bytes 1179656 | tf_op jit(solution)/shard_map/ppermute | solution.py:37
  117.2 20.4 %collective-permute-start.14 = (bf16[8,32,768]{2,1,0:T(8,128)(2,1)S(1)}, bf16[8,32,768]{2,1,0:T(8,128)(2,1)}, u32[]{:S(2)}, u32[]{:S(2)}) collective-permute-start(bf16[8,32,768]{2,1,0:T(8,128)(2,1)S(1)} %copy.66), channel_id=1, source_target_pairs={{0,4},{4,8},{8,12},{12,16},{16,20},{20,24},{24,28},{28,0},{1,5},{5... | collective-permute-start | bytes 1179656 | tf_op jit(solution)/shard_map/ppermute | solution.py:37
  119.7 38.7 %collective-permute-start.9 = (bf16[8,32,768]{2,1,0:T(8,128)(2,1)}, bf16[8,32,768]{2,1,0:T(8,128)(2,1)}, u32[]{:S(2)}, u32[]{:S(2)}) collective-permute-start(bf16[8,32,768]{2,1,0:T(8,128)(2,1)} %collective-permute-done.8), channel_id=1, source_target_pairs={{0,4},{4,8},{8,12},{12,16},{16,20},{20,24},{24,28},{28,0},{1,5},{5... | collective-permute-start | bytes 1179656 | tf_op jit(solution)/shard_map/ppermute | solution.py:37
  128.1 38.7 %collective-permute-start.3 = (bf16[8,32,768]{2,1,0:T(8,128)(2,1)}, bf16[8,32,768]{2,1,0:T(8,128)(2,1)}, u32[]{:S(2)}, u32[]{:S(2)}) collective-permute-start(bf16[8,32,768]{2,1,0:T(8,128)(2,1)} %collective-permute-done.2), channel_id=1, source_target_pairs={{0,4},{4,8},{8,12},{12,16},{16,20},{20,24},{24,28},{28,0},{1,5},{5... | collective-permute-start | bytes 1179656 | tf_op jit(solution)/shard_map/ppermute | solution.py:37
  132.8 53.4 %collective-permute-start.25 = (bf16[8,32,768]{2,1,0:T(8,128)(2,1)S(1)}, bf16[8,32,768]{2,1,0:T(8,128)(2,1)S(1)}, u32[]{:S(2)}, u32[]{:S(2)}) collective-permute-start(bf16[8,32,768]{2,1,0:T(8,128)(2,1)S(1)} %copy.73), channel_id=1, source_target_pairs={{0,28},{4,0},{8,4},{12,8},{16,12},{20,16},{24,20},{28,24},{1,29},{... | collective-permute-start | bytes 1179656 | tf_op jit(solution)/shard_map/ppermute | solution.py:39
  137.6 49.4 %collective-permute-start.21 = (bf16[8,32,768]{2,1,0:T(8,128)(2,1)S(1)}, bf16[8,32,768]{2,1,0:T(8,128)(2,1)S(1)}, u32[]{:S(2)}, u32[]{:S(2)}) collective-permute-start(bf16[8,32,768]{2,1,0:T(8,128)(2,1)S(1)} %copy.73), channel_id=1, source_target_pairs={{0,4},{4,8},{8,12},{12,16},{16,20},{20,24},{24,28},{28,0},{1,5},{5... | collective-permute-start | bytes 1179656 | tf_op jit(solution)/shard_map/ppermute | solution.py:37
  137.6 57.1 %collective-permute-start.18 = (bf16[8,32,768]{2,1,0:T(8,128)(2,1)S(1)}, bf16[8,32,768]{2,1,0:T(8,128)(2,1)S(1)}, u32[]{:S(2)}, u32[]{:S(2)}) collective-permute-start(bf16[8,32,768]{2,1,0:T(8,128)(2,1)S(1)} %copy.66), channel_id=1, source_target_pairs={{0,28},{4,0},{8,4},{12,8},{16,12},{20,16},{24,20},{28,24},{1,29},{... | collective-permute-start | bytes 1179656 | tf_op jit(solution)/shard_map/ppermute | solution.py:39
  158.3 37.0 %collective-permute-start.15 = (bf16[8,32,768]{2,1,0:T(8,128)(2,1)}, bf16[8,32,768]{2,1,0:T(8,128)(2,1)S(1)}, u32[]{:S(2)}, u32[]{:S(2)}) collective-permute-start(bf16[8,32,768]{2,1,0:T(8,128)(2,1)} %collective-permute-done.14), channel_id=1, source_target_pairs={{0,4},{4,8},{8,12},{12,16},{16,20},{20,24},{24,28},{28,0},{1,5},{5... | collective-permute-start | bytes 1179656 | tf_op jit(solution)/shard_map/ppermute | solution.py:37
  166.8 50.6 %collective-permute-start.10 = (bf16[8,32,768]{2,1,0:T(8,128)(2,1)}, bf16[8,32,768]{2,1,0:T(8,128)(2,1)}, u32[]{:S(2)}, u32[]{:S(2)}) collective-permute-start(bf16[8,32,768]{2,1,0:T(8,128)(2,1)} %collective-permute-done.9), channel_id=1, source_target_pairs={{0,4},{4,8},{8,12},{12,16},{16,20},{20,24},{24,28},{28,0},{1,5},{5... | collective-permute-start | bytes 1179656 | tf_op jit(solution)/shard_map/ppermute | solution.py:37
  186.2 38.9 %collective-permute-start.11 = (bf16[8,32,768]{2,1,0:T(8,128)(2,1)S(1)}, bf16[8,32,768]{2,1,0:T(8,128)(2,1)S(1)}, u32[]{:S(2)}, u32[]{:S(2)}) collective-permute-start(bf16[8,32,768]{2,1,0:T(8,128)(2,1)S(1)} %copy.59), channel_id=1, source_target_pairs={{0,28},{4,0},{8,4},{12,8},{16,12},{20,16},{24,20},{28,24},{1,29},{... | collective-permute-start | bytes 1179656 | tf_op jit(solution)/shard_map/ppermute | solution.py:39
  186.9 41.3 %collective-permute-start.4 = (bf16[8,32,768]{2,1,0:T(8,128)(2,1)S(1)}, bf16[8,32,768]{2,1,0:T(8,128)(2,1)S(1)}, u32[]{:S(2)}, u32[]{:S(2)}) collective-permute-start(bf16[8,32,768]{2,1,0:T(8,128)(2,1)S(1)} %copy-done.6), channel_id=1, source_target_pairs={{0,28},{4,0},{8,4},{12,8},{16,12},{20,16},{24,20},{28,24},{1,29},{... | collective-permute-start | bytes 1179656 | tf_op jit(solution)/shard_map/ppermute | solution.py:39
  194.7 42.1 %collective-permute-start.26 = (bf16[8,32,768]{2,1,0:T(8,128)(2,1)S(1)}, bf16[8,32,768]{2,1,0:T(8,128)(2,1)S(1)}, u32[]{:S(2)}, u32[]{:S(2)}) collective-permute-start(bf16[8,32,768]{2,1,0:T(8,128)(2,1)S(1)} %collective-permute-done.25), channel_id=1, source_target_pairs={{0,28},{4,0},{8,4},{12,8},{16,12},{20,16},{24,20},{28,24},{1,29},{... | collective-permute-start | bytes 1179656 | tf_op jit(solution)/shard_map/ppermute | solution.py:39
  195.3 55.6 %collective-permute-start.22 = (bf16[8,32,768]{2,1,0:T(8,128)(2,1)S(1)}, bf16[8,32,768]{2,1,0:T(8,128)(2,1)S(1)}, u32[]{:S(2)}, u32[]{:S(2)}) collective-permute-start(bf16[8,32,768]{2,1,0:T(8,128)(2,1)S(1)} %collective-permute-done.21), channel_id=1, source_target_pairs={{0,4},{4,8},{8,12},{12,16},{16,20},{20,24},{24,28},{28,0},{1,5},{5... | collective-permute-start | bytes 1179656 | tf_op jit(solution)/shard_map/ppermute | solution.py:37
  217.3 42.0 %collective-permute-start.16 = (bf16[8,32,768]{2,1,0:T(8,128)(2,1)S(1)}, bf16[8,32,768]{2,1,0:T(8,128)(2,1)S(1)}, u32[]{:S(2)}, u32[]{:S(2)}) collective-permute-start(bf16[8,32,768]{2,1,0:T(8,128)(2,1)S(1)} %collective-permute-done.15), channel_id=1, source_target_pairs={{0,4},{4,8},{8,12},{12,16},{16,20},{20,24},{24,28},{28,0},{1,5},{5... | collective-permute-start | bytes 1179656 | tf_op jit(solution)/shard_map/ppermute | solution.py:37
  225.1 87.7 %copy-start.7 = (bf16[8,32,768]{2,1,0:T(8,128)(2,1)}, bf16[8,32,768]{2,1,0:T(8,128)(2,1)S(1)}, u32[]{:S(2)}) copy-start(bf16[8,32,768]{2,1,0:T(8,128)(2,1)S(1)} %collective-permute-done.11) | copy-start | bytes 1179652
  225.1 39.8 %collective-permute-start.19 = (bf16[8,32,768]{2,1,0:T(8,128)(2,1)S(1)}, bf16[8,32,768]{2,1,0:T(8,128)(2,1)S(1)}, u32[]{:S(2)}, u32[]{:S(2)}) collective-permute-start(bf16[8,32,768]{2,1,0:T(8,128)(2,1)S(1)} %collective-permute-done.18), channel_id=1, source_target_pairs={{0,28},{4,0},{8,4},{12,8},{16,12},{20,16},{24,20},{28,24},{1,29},{... | collective-permute-start | bytes 1179656 | tf_op jit(solution)/shard_map/ppermute | solution.py:39
  228.2 84.6 %copy-start.9 = (bf16[8,32,768]{2,1,0:T(8,128)(2,1)}, bf16[8,32,768]{2,1,0:T(8,128)(2,1)S(1)}, u32[]{:S(2)}) copy-start(bf16[8,32,768]{2,1,0:T(8,128)(2,1)S(1)} %collective-permute-done.4) | copy-start | bytes 1179652
  228.2 39.8 %collective-permute-start.12 = (bf16[8,32,768]{2,1,0:T(8,128)(2,1)S(1)}, bf16[8,32,768]{2,1,0:T(8,128)(2,1)}, u32[]{:S(2)}, u32[]{:S(2)}) collective-permute-start(bf16[8,32,768]{2,1,0:T(8,128)(2,1)S(1)} %collective-permute-done.11), channel_id=1, source_target_pairs={{0,28},{4,0},{8,4},{12,8},{16,12},{20,16},{24,20},{28,24},{1,29},{... | collective-permute-start | bytes 1179656 | tf_op jit(solution)/shard_map/ppermute | solution.py:39
  236.8 42.2 %collective-permute-start.5 = (bf16[8,32,768]{2,1,0:T(8,128)(2,1)S(1)}, bf16[8,32,768]{2,1,0:T(8,128)(2,1)}, u32[]{:S(2)}, u32[]{:S(2)}) collective-permute-start(bf16[8,32,768]{2,1,0:T(8,128)(2,1)S(1)} %collective-permute-done.4), channel_id=1, source_target_pairs={{0,28},{4,0},{8,4},{12,8},{16,12},{20,16},{24,20},{28,24},{1,29},{... | collective-permute-start | bytes 1179656 | tf_op jit(solution)/shard_map/ppermute | solution.py:39
  250.9 42.1 %collective-permute-start.23 = (bf16[8,32,768]{2,1,0:T(8,128)(2,1)S(1)}, bf16[8,32,768]{2,1,0:T(8,128)(2,1)S(1)}, u32[]{:S(2)}, u32[]{:S(2)}) collective-permute-start(bf16[8,32,768]{2,1,0:T(8,128)(2,1)S(1)} %collective-permute-done.22), channel_id=1, source_target_pairs={{0,4},{4,8},{8,12},{12,16},{16,20},{20,24},{24,28},{28,0},{1,5},{5... | collective-permute-start | bytes 1179656 | tf_op jit(solution)/shard_map/ppermute | solution.py:37
  259.3 49.4 %collective-permute-start.17 = (bf16[8,32,768]{2,1,0:T(8,128)(2,1)S(1)}, bf16[8,32,768]{2,1,0:T(8,128)(2,1)S(1)}, u32[]{:S(2)}, u32[]{:S(2)}) collective-permute-start(bf16[8,32,768]{2,1,0:T(8,128)(2,1)S(1)} %collective-permute-done.16), channel_id=1, source_target_pairs={{0,4},{4,8},{8,12},{12,16},{16,20},{20,24},{24,28},{28,0},{1,5},{5... | collective-permute-start | bytes 1179656 | tf_op jit(solution)/shard_map/ppermute | solution.py:37
  265.0 57.4 %collective-permute-start.27 = (bf16[8,32,768]{2,1,0:T(8,128)(2,1)S(1)}, bf16[8,32,768]{2,1,0:T(8,128)(2,1)S(1)}, u32[]{:S(2)}, u32[]{:S(2)}) collective-permute-start(bf16[8,32,768]{2,1,0:T(8,128)(2,1)S(1)} %collective-permute-done.26), channel_id=1, source_target_pairs={{0,28},{4,0},{8,4},{12,8},{16,12},{20,16},{24,20},{28,24},{1,29},{... | collective-permute-start | bytes 1179656 | tf_op jit(solution)/shard_map/ppermute | solution.py:39
  268.1 54.2 %collective-permute-start.20 = (bf16[8,32,768]{2,1,0:T(8,128)(2,1)S(1)}, bf16[8,32,768]{2,1,0:T(8,128)(2,1)S(1)}, u32[]{:S(2)}, u32[]{:S(2)}) collective-permute-start(bf16[8,32,768]{2,1,0:T(8,128)(2,1)S(1)} %collective-permute-done.19), channel_id=1, source_target_pairs={{0,28},{4,0},{8,4},{12,8},{16,12},{20,16},{24,20},{28,24},{1,29},{... | collective-permute-start | bytes 1179656 | tf_op jit(solution)/shard_map/ppermute | solution.py:39
  279.0 95.9 %collective-permute-start.13 = (bf16[8,32,768]{2,1,0:T(8,128)(2,1)}, bf16[8,32,768]{2,1,0:T(8,128)(2,1)}, u32[]{:S(2)}, u32[]{:S(2)}) collective-permute-start(bf16[8,32,768]{2,1,0:T(8,128)(2,1)} %collective-permute-done.12), channel_id=1, source_target_pairs={{0,28},{4,0},{8,4},{12,8},{16,12},{20,16},{24,20},{28,24},{1,29},{... | collective-permute-start | bytes 1179656 | tf_op jit(solution)/shard_map/ppermute | solution.py:39
  293.0 80.1 %collective-permute-start.6 = (bf16[8,32,768]{2,1,0:T(8,128)(2,1)}, bf16[8,32,768]{2,1,0:T(8,128)(2,1)}, u32[]{:S(2)}, u32[]{:S(2)}) collective-permute-start(bf16[8,32,768]{2,1,0:T(8,128)(2,1)} %collective-permute-done.5), channel_id=1, source_target_pairs={{0,28},{4,0},{8,4},{12,8},{16,12},{20,16},{24,20},{28,24},{1,29},{... | collective-permute-start | bytes 1179656 | tf_op jit(solution)/shard_map/ppermute | solution.py:39
  308.8 13.2 %collective-permute-start.24 = (bf16[8,32,768]{2,1,0:T(8,128)(2,1)S(1)}, bf16[8,32,768]{2,1,0:T(8,128)(2,1)S(1)}, u32[]{:S(2)}, u32[]{:S(2)}) collective-permute-start(bf16[8,32,768]{2,1,0:T(8,128)(2,1)S(1)} %collective-permute-done.23), channel_id=1, source_target_pairs={{0,4},{4,8},{8,12},{12,16},{16,20},{20,24},{24,28},{28,0},{1,5},{5... | collective-permute-start | bytes 1179656 | tf_op jit(solution)/shard_map/ppermute | solution.py:37
  (9 other events, 181.1 us)
Sparse Core Ops, SparseCore 0:
  524.4 29.9 reduce-scatter.1
